TPU v7x, 512 devices: a whole 4x4x16 slice. The times are simulated.
512 devices in a mesh: pipe: 32 (over z, x_hi), tensor: 16 (over x_lo, y, core).
Axes of the slice: x: 4 (x_hi: 2, x_lo: 2; x = x_hi * 2 + x_lo), y: 4, z: 16, core: 2. Of those that a mesh axis runs over, the one named last changes fastest.
Arguments:
- x_saved: bfloat16 [32, 2, 4096, 128], P('pipe', None, 'tensor'), may hold values from -6 to 6
- seed_grad: bfloat16 [32, 2, 4096, 128], P('pipe', None, 'tensor'), may hold values from -6 to 6
- gate_blocks: bfloat16 [32, 16, 7, 20, 4096], P('pipe', 'tensor'), may hold values from -0.1875 to 0.1875
- up_blocks: bfloat16 [32, 16, 7, 20, 4096], P('pipe', 'tensor'), may hold values from -0.1875 to 0.1875
- down_blocks: bfloat16 [32, 16, 7, 20, 4096], P('pipe', 'tensor'), may hold values from -0.1875 to 0.1875
- gate_rows: int32 [32, 16, 7, 20], P('pipe', 'tensor'), may hold values from -1 to 63, as said below
- down_rows: int32 [32, 16, 7, 20], P('pipe', 'tensor'), may hold values from -1 to 63, as said below
Outputs:
- grad_input: bfloat16 [32, 2, 4096, 128], P('pipe', None, 'tensor')
Inputs may be any that keep to these rules, and one draw needn't show every extreme that they name: `gate_rows`: in one column of tiles the non-negative entries are distinct and come before the -1 entries. All columns of one tensor shard of one section hold the same number of kept tiles, from 12 to 20, and in every section one shard holds 20 in every column. `down_rows`: as for gate_rows, drawn independently.
All inputs are finite; a program needn't handle non-finite values.
Results may differ from a plain program's by a relative error of at most 0.007.
Values may be sent and summed in bfloat16 or wider, within the bound.
No kernel may reach another device: no remote copies, remote signals or barrier semaphores. Data moves between devices by JAX's collectives and lax.ppermute only.
A program may use at most 128 MiB of HBM per device.

v0:
```python
import jax
import jax.numpy as jnp
from jax import lax
from jax.sharding import PartitionSpec as P

BLK = 64


def partner_2(x, axis, distance):
    return lax.ppermute(x, axis, [(i, i ^ 1 << distance) for i in range(lax.axis_size(axis))])


def from_behind(block, axis, distance):
    devices = range(lax.axis_size(axis))
    route = [(i - distance, i) for i in devices if i - distance in devices]
    return lax.ppermute(block, axis, route)


def gather_tiles(source, row_ids):
    columns, slot_depth = row_ids.shape
    filled = (row_ids >= 0).reshape(-1)
    picked = jnp.take(source, jnp.maximum(row_ids, 0).reshape(-1), axis=0)
    picked = jnp.where(filled[:, None, None], picked, jnp.zeros_like(picked))
    return picked.reshape(columns, slot_depth, source.shape[1], source.shape[2])


def layer_branch(x_full, cot_full, paired_grid, down_grid, gate_ids, down_ids):
    row_blocks = x_full.shape[0] // BLK
    tokens_now = x_full.shape[1]
    columns, slot_depth = gate_ids.shape
    x_picked = gather_tiles(x_full.reshape(row_blocks, BLK, tokens_now), gate_ids)
    both_values = jnp.einsum(
        "crkj,crkt->cjt", paired_grid, x_picked, preferred_element_type=jnp.float32
    )
    gate_value = both_values[:, :BLK]
    up_value = both_values[:, BLK:]
    cot_picked = gather_tiles(cot_full.reshape(row_blocks, BLK, tokens_now), down_ids)
    d_hidden = jnp.einsum(
        "crjk,crkt->cjt", down_grid, cot_picked, preferred_element_type=jnp.float32
    )
    sigmoid_gate = jax.nn.sigmoid(gate_value)
    d_gate = (
        d_hidden * up_value * sigmoid_gate * (1.0 + gate_value * (1.0 - sigmoid_gate))
    ).astype(jnp.bfloat16)
    d_up = (d_hidden * gate_value * sigmoid_gate).astype(jnp.bfloat16)
    d_both = jnp.concatenate([d_gate, d_up], axis=1)
    per_slot = jnp.einsum("crkj,cjt->crkt", paired_grid, d_both, preferred_element_type=jnp.float32)
    segment_ids = jnp.where(gate_ids >= 0, gate_ids, row_blocks).reshape(-1)
    summed = jax.ops.segment_sum(
        per_slot.reshape(columns * slot_depth, BLK, tokens_now),
        segment_ids,
        num_segments=row_blocks + 1,
    )
    return summed[:row_blocks].reshape(row_blocks * BLK, tokens_now)


def per_device(x_saved, seed_grad, gate_blocks, up_blocks, down_blocks, gate_rows, down_rows):
    pipe_index = lax.axis_index("pipe")
    pair_half = pipe_index % 2
    last_section = pipe_index // 2 == lax.axis_size("pipe") // 2 - 1
    own_parts = (gate_blocks, up_blocks, down_blocks, gate_rows, down_rows)
    partner = partner_2((gate_blocks, up_blocks, down_blocks, gate_rows, down_rows), "pipe", 0)
    joined = []
    for own_part, theirs in zip(own_parts, partner):
        first_half = jnp.where(pair_half == 0, own_part, theirs)
        second_half = jnp.where(pair_half == 0, theirs, own_part)
        joined.append(jnp.concatenate([first_half[0, 0], second_half[0, 0]], axis=0))
    gate_set, up_set, down_set, gate_ids, down_ids = joined
    columns, slot_depth = gate_ids.shape
    tile_shape = (columns, slot_depth, BLK, BLK)
    paired_grid = jnp.concatenate(
        [gate_set.reshape(tile_shape), up_set.reshape(tile_shape)], axis=3
    )
    down_grid = down_set.reshape(tile_shape)
    panel_rows = x_saved.shape[2]
    micro_total = x_saved.shape[1]
    arrived = None
    grads = []
    for micro_step in range(micro_total):
        x_panel = x_saved[0, micro_step]
        seed_panel = seed_grad[0, micro_step]
        x_full, cot_full = (
            lax.all_gather(x_panel, "tensor", axis=0, tiled=True),
            lax.all_gather(seed_panel, "tensor", axis=0, tiled=True),
        )
        if micro_step > 0:
            cot_full = jnp.where(last_section, cot_full, arrived)
        branch = layer_branch(x_full, cot_full, paired_grid, down_grid, gate_ids, down_ids)
        summed = lax.psum(branch, "tensor")
        grad_full = (cot_full.astype(jnp.float32) + summed).astype(jnp.bfloat16)
        grad_panel = lax.dynamic_slice_in_dim(
            grad_full, lax.axis_index("tensor") * panel_rows, panel_rows, 0
        )
        if micro_step + 1 < micro_total:
            arrived = from_behind(grad_full, "pipe", -2)
        grads.append(grad_panel)
    return jnp.stack(grads)[None]


def solution(mesh):
    return jax.shard_map(
        per_device,
        mesh=mesh,
        in_specs=(
            P("pipe", None, "tensor", None),
            P("pipe", None, "tensor", None),
            P("pipe", "tensor", None, None, None),
            P("pipe", "tensor", None, None, None),
            P("pipe", "tensor", None, None, None),
            P("pipe", "tensor", None, None),
            P("pipe", "tensor", None, None),
        ),
        out_specs=P("pipe", None, "tensor", None),
        check_vma=False,
    )
```

profile of v0, /device:TPU:6, one launch (start us, length us, event | category | flops | bytes accessed | tf_op | source)
XLA Modules:
  0.0 602.2 jit_solution(8425488830314063497)
XLA Ops:
  9.6 3.3 collective-permute-start
  12.9 4.0 collective-permute-start.4
  16.9 3.3 collective-permute-start.3
  20.3 4.0 collective-permute-start.2
  24.3 3.3 collective-permute-start.1
  31.3 25.9 %collective-permute-done.3 = bf16[1,1,7,20,4096]{4,2,3,1,0:T(8,128)(2,1)S(1)} collective-permute-done((bf16[1,1,7,20,4096]{4,2,3,1,0:T(8,128)(2,1)}, bf16[1,1,7,20,4096]{4,2,3,1,0:T(8,128)(2,1)S(1)}, u32[]{:S(2)}, u32[]{:S(2)}) %collective-permute-start.3) | collective-permute-done | bytes 1146912 | tf_op jit(solution)/shard_map/ppermute | solution.py:10
  57.2 31.2 %collective-permute-done.2 = bf16[1,1,7,20,4096]{4,2,3,1,0:T(8,128)(2,1)S(1)} collective-permute-done((bf16[1,1,7,20,4096]{4,2,3,1,0:T(8,128)(2,1)}, bf16[1,1,7,20,4096]{4,2,3,1,0:T(8,128)(2,1)S(1)}, u32[]{:S(2)}, u32[]{:S(2)}) %collective-permute-start.2) | collective-permute-done | bytes 1146912 | tf_op jit(solution)/shard_map/ppermute | solution.py:10
  88.4 4.2 broadcast_select_fusion.1
  92.6 3.6 concatenate.47
  96.1 4.5 concatenate.46
  100.7 15.9 %collective-permute-done.1 = bf16[1,1,7,20,4096]{4,2,3,1,0:T(8,128)(2,1)} collective-permute-done((bf16[1,1,7,20,4096]{4,2,3,1,0:T(8,128)(2,1)}, bf16[1,1,7,20,4096]{4,2,3,1,0:T(8,128)(2,1)}, u32[]{:S(2)}, u32[]{:S(2)}) %collective-permute-start.1) | collective-permute-done | bytes 1146912 | tf_op jit(solution)/shard_map/ppermute | solution.py:10
  116.6 3.3 broadcast_select_fusion.5
  120.0 4.5 concatenate.44
  124.5 4.5 concatenate.43
  129.0 4.5 concatenate.51
  133.6 4.5 concatenate.50
  138.1 6.3 %maximum_maximum_fusion = bf16[14,20,64,128]{3,2,0,1:T(8,128)(2,1)} fusion(bf16[7,20,64,64]{3,2,0,1:T(8,128)(2,1)S(1)} %concatenate.47, bf16[7,20,64,64]{3,2,0,1:T(8,128)(2,1)} %concatenate.46, bf16[7,20,64,64]{3,2,0,1:T(8,128)(2,1)} %concatenate.44, bf16[7,20,64,64]{3,2,0,1:T(8,128)(2,1)} %concatenate.43), kind=kLoop, calls=%fused_computation.6 | loop fusion | flops 18350080 | bytes 9175040 | tf_op jit(solution)/shard_map/concatenate | solution.py:71
  144.4 4.6 gather_fusion.3
  149.1 4.7 gather_fusion.1
  153.8 7.8 %select_select_fusion = (bf16[280,64,128]{2,1,0:T(8,128)(2,1)}, bf16[280,64,128]{2,1,0:T(8,128)(2,1)S(1)}) fusion(bf16[280,64,128]{2,1,0:T(8,128)(2,1)} %gather_fusion.3, pred[280]{0:T(512)(128)(4,1)S(1)} %compare_and_fusion, pred[280]{0:T(512)(128)(4,1)S(1)} %ge.42, bf16[280,64,128]{2,1,0:T(8,128)(2,1)} %gather_fusion.1), kind=kLoop, calls=%fused_computation.8 | loop fusion | flops 9175040 | bytes 18350640 | tf_op jit(solution)/shard_map/jit(_where)/select_n | solution.py:23
  163.1 4.7 gather_fusion
  167.8 4.7 select_select_fusion.3
  174.6 4.9 fusion.8
  179.8 29.7 %scatter_fusion = f32[65,64,128]{2,1,0:T(8,128)S(1)} fusion(f32[65,64,128]{2,1,0:T(8,128)S(1)} %broadcast.48.clone, s32[280]{0:T(512)S(1)} %fusion.40, f32[280,64,128]{2,1,0:T(8,128)} %bitcast.77), kind=kCustom, calls=%fused_computation.4 | custom fusion | flops 2293760 | bytes 27526240 | tf_op jit(solution)/shard_map/scatter-add | solution.py:49
  211.6 142.1 %all-reduce.3.cloned.1.call-done = f32[4096,128]{1,0:T(8,128)} async-done(((f32[4096,128]{1,0:T(8,128)}), f32[4096,128]{1,0:T(8,128)}) %all-reduce.3.cloned.1.call-update) | async-done | bytes 2097168 | tf_op jit(solution)/shard_map/psum | solution.py:89
  356.8 6.1 %fusion.16 = f32[14,128,128]{2,1,0:T(8,128)} fusion(bf16[14,20,64,128]{3,2,1,0:T(8,128)(2,1)} %bitcast.84, bf16[14,20,64,128]{3,2,0,1:T(8,128)(2,1)} %maximum_maximum_fusion), kind=kOutput, calls=%fused_computation.27 | convolution fusion | flops 587202560 | bytes 10092544 | tf_op jit(solution)/shard_map/crkj,crkt->cjt/dot_general | solution.py:32
  362.9 34.3 %all-gather.13.cloned.1.call-done = bf16[1,1,4096,128]{3,2,1,0:T(8,128)(2,1)} async-done(((bf16[1,1,256,128]{3,2,1,0:T(8,128)(2,1)}), bf16[1,1,4096,128]{3,2,1,0:T(8,128)(2,1)}) %all-gather.13.cloned.1.call-update) | async-done | bytes 1048592 | tf_op jit(solution)/shard_map/all_gather | solution.py:84
  398.5 13.6 %gather_fusion.2 = bf16[280,64,128]{2,1,0:T(8,128)(2,1)} fusion(bf16[64,64,128]{2,1,0:T(8,128)(2,1)S(1)} %bitcast.78, s32[1024]{0:T(1024)S(1)} %pad_clamp_fusion.1), kind=kCustom, calls=%fused_computation.2.clone | custom fusion | bytes 9176160 | tf_op jit(solution)/shard_map/jit(_take)/gather | solution.py:22
  412.1 4.7 select_select_fusion.1
  418.9 4.9 fusion.4
  424.1 29.7 %scatter_fusion.1 = f32[65,64,128]{2,1,0:T(8,128)S(1)} fusion(f32[65,64,128]{2,1,0:T(8,128)S(1)} %broadcast.48, s32[280]{0:T(512)S(1)} %fusion.40, f32[280,64,128]{2,1,0:T(8,128)} %bitcast.76), kind=kCustom, calls=%fused_computation.5 | custom fusion | flops 2293760 | bytes 27526240 | tf_op jit(solution)/shard_map/scatter-add | solution.py:49
  456.1 137.6 %all-reduce.5.cloned.1.call-done = f32[4096,128]{1,0:T(8,128)} async-done(((f32[4096,128]{1,0:T(8,128)}), f32[4096,128]{1,0:T(8,128)}) %all-reduce.5.cloned.1.call-update) | async-done | bytes 2097168 | tf_op jit(solution)/shard_map/psum | solution.py:89
  (82 shorter events, 23.1 us)
Async XLA Ops:
  6.5 137.9 %all-gather.15.cloned.1.call-start = ((), (), s32[]{:S(2)}) async-start(), calls=%async_computation.5 | async-start | bytes 1114112 | tf_op jit(solution)/shard_map/all_gather | solution.py:83
  8.1 141.0 %all-gather.11.cloned.1.call-start = ((), (), s32[]{:S(2)}) async-start(), calls=%async_computation.3 | async-start | bytes 1114112 | tf_op jit(solution)/shard_map/all_gather | solution.py:83
  8.8 154.3 %all-gather.9.cloned.1.call-start = ((), (), s32[]{:S(2)}) async-start(), calls=%async_computation.2 | async-start | bytes 1114112 | tf_op jit(solution)/shard_map/all_gather | solution.py:84
  9.6 19.7 %collective-permute-start = (s32[1,1,7,20]{3,2,1,0:T(8,128)S(1)}, s32[1,1,7,20]{3,2,1,0:T(8,128)S(1)}, u32[]{:S(2)}, u32[]{:S(2)}) collective-permute-start(s32[1,1,7,20]{3,2,1,0:T(8,128)S(1)} %copy.21), channel_id=1, source_target_pairs={{0,16},{16,0},{32,48},{48,32},{64,80},{80,64},{96,112},{112,96},{1... | collective-permute-start | bytes 1688 | tf_op jit(solution)/shard_map/ppermute | solution.py:10
  12.9 16.4 %collective-permute-start.4 = (s32[1,1,7,20]{3,1,2,0:T(1,128)}, s32[1,1,7,20]{3,1,2,0:T(1,128)S(1)}, u32[]{:S(2)}, u32[]{:S(2)}) collective-permute-start(s32[1,1,7,20]{3,1,2,0:T(1,128)} %param.15), channel_id=1, source_target_pairs={{0,16},{16,0},{32,48},{48,32},{64,80},{80,64},{96,112},{112,96},{1... | collective-permute-start | bytes 1688 | tf_op jit(solution)/shard_map/ppermute | solution.py:10
  16.9 40.2 %collective-permute-start.3 = (bf16[1,1,7,20,4096]{4,2,3,1,0:T(8,128)(2,1)}, bf16[1,1,7,20,4096]{4,2,3,1,0:T(8,128)(2,1)S(1)}, u32[]{:S(2)}, u32[]{:S(2)}) collective-permute-start(bf16[1,1,7,20,4096]{4,2,3,1,0:T(8,128)(2,1)} %param.13), channel_id=1, source_target_pairs={{0,16},{16,0},{32,48},{48,32},{64,80},{80,64},{96,112},{112,96},{1... | collective-permute-start | bytes 3440648 | tf_op jit(solution)/shard_map/ppermute | solution.py:10
  20.3 68.1 %collective-permute-start.2 = (bf16[1,1,7,20,4096]{4,2,3,1,0:T(8,128)(2,1)}, bf16[1,1,7,20,4096]{4,2,3,1,0:T(8,128)(2,1)S(1)}, u32[]{:S(2)}, u32[]{:S(2)}) collective-permute-start(bf16[1,1,7,20,4096]{4,2,3,1,0:T(8,128)(2,1)} %param.12), channel_id=1, source_target_pairs={{0,16},{16,0},{32,48},{48,32},{64,80},{80,64},{96,112},{112,96},{1... | collective-permute-start | bytes 3440648 | tf_op jit(solution)/shard_map/ppermute | solution.py:10
  24.3 92.3 %collective-permute-start.1 = (bf16[1,1,7,20,4096]{4,2,3,1,0:T(8,128)(2,1)}, bf16[1,1,7,20,4096]{4,2,3,1,0:T(8,128)(2,1)}, u32[]{:S(2)}, u32[]{:S(2)}) collective-permute-start(bf16[1,1,7,20,4096]{4,2,3,1,0:T(8,128)(2,1)} %param.11), channel_id=1, source_target_pairs={{0,16},{16,0},{32,48},{48,32},{64,80},{80,64},{96,112},{112,96},{1... | collective-permute-start | bytes 3440648 | tf_op jit(solution)/shard_map/ppermute | solution.py:10
  29.2 324.5 %all-reduce.3.cloned.1.call-start = ((), (), s32[]{:S(2)}) async-start(), calls=%async_computation | async-start | bytes 4194304 | tf_op jit(solution)/shard_map/psum | solution.py:89
  149.1 12.5 %slice-start = ((s8[4587520]{0:T(1024)(128)(4,1)}), s8[393216]{0:T(1024)(128)(4,1)S(1)}, s32[]{:S(2)}) async-start(s8[4587520]{0:T(1024)(128)(4,1)} %bitcast.70), calls=%async_computation.6 | async-start | bytes 786432
  153.8 7.8 %slice-start.1 = ((s8[4587520]{0:T(1024)(128)(4,1)}), s8[4194304]{0:T(1024)(128)(4,1)S(1)}, s32[]{:S(2)}) async-start(s8[4587520]{0:T(1024)(128)(4,1)} %bitcast.70), calls=%async_computation.7 | async-start | bytes 8388608
  167.8 4.7 copy-start.1
  167.8 4.7 copy-start.3
  167.8 6.8 %slice-start.2 = ((s8[4587520]{0:T(1024)(128)(4,1)}), s8[4194304]{0:T(1024)(128)(4,1)S(1)}, s32[]{:S(2)}) async-start(s8[4587520]{0:T(1024)(128)(4,1)} %bitcast.72), calls=%async_computation.8 | async-start | bytes 8388608
  172.6 2.0 slice-start.3
  209.5 144.2 %copy-start = (bf16[1,1,4096,128]{3,2,1,0:T(8,128)(2,1)S(1)}, bf16[1,1,4096,128]{3,2,1,0:T(8,128)(2,1)}, u32[]{:S(2)}) copy-start(bf16[1,1,4096,128]{3,2,1,0:T(8,128)(2,1)} %all-gather.9.cloned.1.call-done) | copy-start | bytes 3145732
  211.0 186.2 %all-gather.13.cloned.1.call-start = ((), (), s32[]{:S(2)}) async-start(), calls=%async_computation.4 | async-start | bytes 1114112 | tf_op jit(solution)/shard_map/all_gather | solution.py:84
  211.6 382.2 %all-reduce.5.cloned.1.call-start = ((), (), s32[]{:S(2)}) async-start(), calls=%async_computation.1 | async-start | bytes 4194304 | tf_op jit(solution)/shard_map/psum | solution.py:89
  355.5 7.4 %copy-start.5 = (bf16[4096,128]{1,0:T(8,128)(2,1)}, bf16[4096,128]{1,0:T(8,128)(2,1)S(1)}, u32[]{:S(2)}) copy-start(bf16[4096,128]{1,0:T(8,128)(2,1)S(1)} %fusion.12) | copy-start | bytes 3145732
  355.5 41.7 %collective-permute-start.5 = (bf16[4096,128]{1,0:T(8,128)(2,1)S(1)}, bf16[4096,128]{1,0:T(8,128)(2,1)S(1)}, u32[]{:S(2)}, u32[]{:S(2)}) collective-permute-start(bf16[4096,128]{1,0:T(8,128)(2,1)S(1)} %fusion.12), channel_id=1, source_target_pairs={{32,0},{48,16},{64,32},{80,48},{96,64},{112,80},{128,96},{144,112}... | collective-permute-start | bytes 3145736 | tf_op jit(solution)/shard_map/ppermute | solution.py:16
  398.5 18.3 %copy-start.6 = (f32[14,128,128]{2,1,0:T(8,128)S(1)}, f32[14,128,128]{2,1,0:T(8,128)}, u32[]{:S(2)}) copy-start(f32[14,128,128]{2,1,0:T(8,128)} %fusion.16) | copy-start | bytes 2752516
  412.1 4.8 copy-start.2
  412.1 4.8 copy-start.4
  412.1 6.8 %slice-start.4 = ((s8[4587520]{0:T(1024)(128)(4,1)}), s8[4194304]{0:T(1024)(128)(4,1)S(1)}, s32[]{:S(2)}) async-start(s8[4587520]{0:T(1024)(128)(4,1)} %bitcast.74), calls=%async_computation.10 | async-start | bytes 8388608
  416.9 2.0 slice-start.5
Sparse Core Ops, SparseCore 0:
  9.5 45.5 all-gather.14
  57.2 41.3 all-gather.10
  100.7 40.6 all-gather.8
  211.1 142.5 all-reduce.2
  355.7 41.4 all-gather.12
  455.4 138.2 all-reduce.4
where the time goes:
time: 606 us; the launch traced here: 602 us
  waiting for transfers between devices  388 us (64%)
  other arithmetic  96.7 us (16%)
  local copies, waits for them, and re-layouts  62.3 us (10%)
  matrix products  21.5 us (4%)
  starting transfers between devices  19.5 us (3%)
  between operations  13.9 us (2%)
    psum x2, waiting for transfers between devices, per_device(): summed = lax.psum(branch, 'tensor')  280 us
    ppermute x5, waiting for transfers between devices, partner_2(): lax.ppermute(x, axis, [(i, i ^ 1 << distance) for i in range(lax.axis_siz...  73 us
    scatter-add x2, other arithmetic, layer_branch(): jax.ops.segment_sum(per_slot.reshape(columns * slot_depth, BLK, tokens_no...  59.3 us
    all_gather x2, waiting for transfers between devices, per_device(): lax.all_gather(seed_panel, 'tensor', axis=0, tiled=True)  34.3 us
    gather x4, local copies, waits for them, and re-layouts, gather_tiles(): picked = jnp.take(source, jnp.maximum(row_ids, 0).reshape(-1), axis=0)  27.5 us
    concatenate x7, local copies, waits for them, and re-layouts, per_device(): jnp.concatenate([first_half[0, 0], second_half[0, 0]], axis=0)  26.3 us
    ppermute x5, starting transfers between devices, partner_2(): lax.ppermute(x, axis, [(i, i ^ 1 << distance) for i in range(lax.axis_siz...  18 us
    select_n x3, other arithmetic, gather_tiles(): picked = jnp.where(filled[:, None, None], picked, jnp.zeros_like(picked))  17.3 us
  transfers between devices with their start and end apart: 12, of which 6 were waited for; matrix products, arithmetic and copies ran while one was open for 12% of the time, Pallas kernels for 0%

commit v1 on v0

v1 whole, which is shorter than its diff:
```python
import jax
import jax.numpy as jnp
from jax import lax
from jax.sharding import PartitionSpec as P

BLK = 64
RS_BITS = (0, 3, 1, 2)


def flip_pairs(axis, bit):
    return [(i, i ^ (1 << bit)) for i in range(lax.axis_size(axis))]


def from_behind(block, axis, distance):
    devices = range(lax.axis_size(axis))
    route = [(i - distance, i) for i in devices if i - distance in devices]
    return lax.ppermute(block, axis, route)


def reduce_scatter_tensor(value):
    t = lax.axis_index("tensor")
    n_bits = lax.axis_size("tensor").bit_length() - 1
    rows = value.shape[0] >> n_bits
    cur = value.reshape((2,) * n_bits + (rows, value.shape[1]))
    held = list(range(n_bits - 1, -1, -1))
    for bit in RS_BITS:
        axis = held.index(bit)
        mine = (t >> bit) & 1
        keep = lax.dynamic_index_in_dim(cur, mine, axis, keepdims=False)
        send = lax.dynamic_index_in_dim(cur, 1 - mine, axis, keepdims=False)
        cur = keep + lax.ppermute(send, "tensor", flip_pairs("tensor", bit))
        held.pop(axis)
    return cur


def all_gather_tensor(panel):
    t = lax.axis_index("tensor")
    n_bits = lax.axis_size("tensor").bit_length() - 1
    lead = panel.shape[:-2]
    cur = panel
    held = []
    for bit in reversed(RS_BITS):
        mine = (t >> bit) & 1
        recv = lax.ppermute(cur, "tensor", flip_pairs("tensor", bit))
        lo = jnp.where(mine == 0, cur, recv)
        hi = jnp.where(mine == 0, recv, cur)
        cur = jnp.stack([lo, hi], axis=len(lead))
        held.insert(0, bit)
    order = sorted(range(n_bits), key=lambda i: -held[i])
    lead_n = len(lead)
    perm = list(range(lead_n)) + [lead_n + i for i in order] + [lead_n + n_bits, lead_n + n_bits + 1]
    cur = jnp.transpose(cur, perm)
    return cur.reshape(lead + (panel.shape[-2] << n_bits, panel.shape[-1]))


def dense_in(tiles, row_ids, pattern):
    columns, slot_depth = row_ids.shape
    row_blocks = 64
    onehot = (row_ids[:, :, None] == jnp.arange(row_blocks)[None, None, :]).astype(tiles.dtype)
    grid = tiles.reshape(columns, slot_depth, BLK, BLK)
    dense = jnp.einsum(pattern, onehot, grid, preferred_element_type=jnp.float32)
    return dense.astype(tiles.dtype).reshape(columns * BLK, row_blocks * BLK)


def half_weights(gate_blocks, up_blocks, down_blocks, gate_rows, down_rows):
    wg = dense_in(gate_blocks, gate_rows, "crq,crkj->cjqk")
    wu = dense_in(up_blocks, gate_rows, "crq,crkj->cjqk")
    wd = dense_in(down_blocks, down_rows, "crq,crjk->cjqk")
    return wg, wu, wd


def half_branch(weights, x_full, cot_full):
    wg, wu, wd = weights
    gate_value = jnp.dot(wg, x_full, preferred_element_type=jnp.float32)
    up_value = jnp.dot(wu, x_full, preferred_element_type=jnp.float32)
    d_hidden = jnp.dot(wd, cot_full, preferred_element_type=jnp.float32)
    sigmoid_gate = jax.nn.sigmoid(gate_value)
    d_gate = (
        d_hidden * up_value * sigmoid_gate * (1.0 + gate_value * (1.0 - sigmoid_gate))
    ).astype(jnp.bfloat16)
    d_up = (d_hidden * gate_value * sigmoid_gate).astype(jnp.bfloat16)
    contract = (((0,), (0,)), ((), ()))
    branch = lax.dot_general(wg, d_gate, contract, preferred_element_type=jnp.float32)
    return branch + lax.dot_general(wu, d_up, contract, preferred_element_type=jnp.float32)


def per_device(x_saved, seed_grad, gate_blocks, up_blocks, down_blocks, gate_rows, down_rows):
    pipe_index = lax.axis_index("pipe")
    last_section = pipe_index // 2 == lax.axis_size("pipe") // 2 - 1
    own = tuple(a[0, 0] for a in (gate_blocks, up_blocks, down_blocks, gate_rows, down_rows))
    theirs = lax.ppermute(own, "pipe", flip_pairs("pipe", 0))
    micro_total = x_saved.shape[1]

    first = jnp.stack([x_saved[0, 0], seed_grad[0, 0]])
    x0_full, cot0_full = all_gather_tensor(first)
    own_w = half_weights(*own)
    their_w = half_weights(*theirs)

    grads = []
    cot_full = cot0_full
    x_full = x0_full
    for micro_step in range(micro_total):
        if micro_step > 0:
            x_full = all_gather_tensor(x_saved[0, micro_step])
            arrived = from_behind(grads[-1], "pipe", -2)
            cot_panel = jnp.where(last_section, seed_grad[0, micro_step], arrived)
            cot_full = all_gather_tensor(cot_panel)
        else:
            cot_panel = seed_grad[0, 0]
        branch = half_branch(own_w, x_full, cot_full) + half_branch(their_w, x_full, cot_full)
        summed = reduce_scatter_tensor(branch)
        grads.append((cot_panel.astype(jnp.float32) + summed).astype(jnp.bfloat16))
    return jnp.stack(grads)[None]


def solution(mesh):
    return jax.shard_map(
        per_device,
        mesh=mesh,
        in_specs=(
            P("pipe", None, "tensor", None),
            P("pipe", None, "tensor", None),
            P("pipe", "tensor", None, None, None),
            P("pipe", "tensor", None, None, None),
            P("pipe", "tensor", None, None, None),
            P("pipe", "tensor", None, None),
            P("pipe", "tensor", None, None),
        ),
        out_specs=P("pipe", None, "tensor", None),
        check_vma=False,
    )
```

time: 606 us -> 406 us (0.67)
  waiting for transfers between devices: 388 us -> 57.9 us
  other arithmetic: 96.7 us -> 7 us
  local copies, waits for them, and re-layouts: 62.3 us -> 151 us
  matrix products: 21.5 us -> 97.4 us
  starting transfers between devices: 19.5 us -> 84.3 us
  between operations: 13.9 us -> 1.11 us
    psum x2 -> x0, waiting for transfers between devices: 280 us -> none  [per_device(): summed = lax.psum(branch, 'tensor')]
    dot_general x6 -> x22, matrix products: 21.5 us -> 97.4 us  [the longest x4 35.1 us: half_branch(): lax.dot_general(wg, d_gate, contract, preferred_element_type=jnp.float32)]
    reshape x0 -> x9, local copies, waits for them, and re-layouts: none -> 74.3 us  [the longest x6 63.6 us: dense_in(): return dense.astype(tiles.dtype).reshape(columns * BLK, row_blocks * BLK)]
    ppermute x5 -> x25, starting transfers between devices: 18 us -> 83.1 us  [the longest x12 39.8 us: all_gather_tensor(): recv = lax.ppermute(cur, 'tensor', flip_pairs('tensor', bit))]
    scatter-add x2 -> x0, other arithmetic: 59.3 us -> none  [layer_branch(): jax.ops.segment_sum(per_slot.reshape(columns * slot_depth, BLK, tokens_no...]
    convert_element_type x0 -> x4, local copies, waits for them, and re-layouts: none -> 52.6 us  [dense_in(): return dense.astype(tiles.dtype).reshape(columns * BLK, row_blocks * BLK)]
    all_gather x4 -> x0, waiting for transfers between devices: 34.3 us -> none  [the longest x2 34.3 us: per_device(): lax.all_gather(seed_panel, 'tensor', axis=0, tiled=True)]
    gather x4 -> x0, local copies, waits for them, and re-layouts: 27.5 us -> none  [gather_tiles(): picked = jnp.take(source, jnp.maximum(row_ids, 0).reshape(-1), axis=0)]
  transfers between devices with their start and end apart: 12 -> 26, of which waited for: 6 -> 14; matrix products, arithmetic and copies ran while one was open for 12% -> 45% of each run, Pallas kernels for 0% -> 0%
where the time goes in v1:
time: 406 us; the launch traced here: 398 us
  local copies, waits for them, and re-layouts  151 us (37%)
  matrix products  97.4 us (24%)
  starting transfers between devices  84.3 us (21%)
  waiting for transfers between devices  57.9 us (14%)
  other arithmetic  7 us (2%)
    reshape x6, local copies, waits for them, and re-layouts, dense_in(): return dense.astype(tiles.dtype).reshape(columns * BLK, row_blocks * BLK)  63.6 us
    convert_element_type x4, local copies, waits for them, and re-layouts, dense_in(): return dense.astype(tiles.dtype).reshape(columns * BLK, row_blocks * BLK)  52.6 us
    ppermute x12, starting transfers between devices, all_gather_tensor(): recv = lax.ppermute(cur, 'tensor', flip_pairs('tensor', bit))  39.8 us
    ppermute x8, waiting for transfers between devices, reduce_scatter_tensor(): cur = keep + lax.ppermute(send, 'tensor', flip_pairs('tensor', bit))  39.5 us
    dot_general x4, matrix products, half_branch(): lax.dot_general(wg, d_gate, contract, preferred_element_type=jnp.float32)  35.1 us
    dot_general x6, matrix products, dense_in(): jnp.einsum(pattern, onehot, grid, preferred_element_type=jnp.float32)  35 us
    ppermute x8, starting transfers between devices, reduce_scatter_tensor(): cur = keep + lax.ppermute(send, 'tensor', flip_pairs('tensor', bit))  24.1 us
    ppermute x5, starting transfers between devices, per_device(): theirs = lax.ppermute(own, 'pipe', flip_pairs('pipe', 0))  19.2 us
  transfers between devices with their start and end apart: 26, of which 14 were waited for; matrix products, arithmetic and copies ran while one was open for 45% of the time, Pallas kernels for 0%

profile of v1, /device:TPU:6, one launch (start us, length us, event | category | flops | bytes accessed | tf_op | source)
XLA Modules:
  0.0 398.4 jit_solution(8678852995782206846)
XLA Ops:
  1.8 5.1 %collective-permute-start = (bf16[2,256,128]{2,1,0:T(8,128)(2,1)S(1)}, bf16[2,256,128]{2,1,0:T(8,128)(2,1)S(1)}, u32[]{:S(2)}, u32[]{:S(2)}) collective-permute-start(bf16[2,256,128]{2,1,0:T(8,128)(2,1)S(1)} %pad_maximum_fusion.7), channel_id=1, source_target_pairs={{0,4},{1,5},{2,6},{3,7},{4,0},{5,1},{6,2},{7,3},{8,12},{9,13},{10,... | collective-permute-start | bytes 393224 | tf_op jit(solution)/shard_map/ppermute | solution.py:44
  22.9 4.5 %reshape_squeeze.9 = bf16[7,20,64,64]{3,2,0,1:T(8,128)(2,1)} reshape(bf16[1,1,7,20,4096]{4,2,3,1,0:T(8,128)(2,1)} %param.9) | data formatting | bytes 2293760 | tf_op jit(solution)/shard_map/reshape;squeeze | solution.py:60
  33.8 7.1 %convert_bitcast_fusion.5 = bf16[7,64,64,64]{1,2,3,0:T(8,128)(2,1)} fusion(bf16[7,20,64,64]{3,2,0,1:T(8,128)(2,1)} %reshape_squeeze.9, s32[7,20]{1,0:T(8,128)S(1)} %bitcast.247), kind=kOutput, calls=%fused_computation.5 | convolution fusion | flops 75244288 | bytes 4817456 | tf_op jit(solution)/shard_map/crq,crkj->cjqk/dot_general | solution.py:61
  44.6 5.6 %convert_bitcast_fusion.4 = bf16[7,64,64,64]{3,2,1,0:T(8,128)(2,1)} fusion(bf16[7,20,64,64]{3,2,0,1:T(8,128)(2,1)S(1)} %reshape_squeeze.10, s32[7,20]{1,0:T(8,128)S(1)} %bitcast.250), kind=kOutput, calls=%fused_computation.4 | convolution fusion | flops 75244288 | bytes 4817456 | tf_op jit(solution)/shard_map/crq,crjk->cjqk/dot_general | solution.py:61
  50.2 13.1 %copy.12 = bf16[7,64,64,64]{3,2,1,0:T(8,128)(2,1)} copy(bf16[7,64,64,64]{1,2,3,0:T(8,128)(2,1)} %convert_bitcast_fusion.5) | data formatting | bytes 7340032 | tf_op jit(solution)/shard_map/convert_element_type | solution.py:62
  63.4 10.6 %reshape.50 = bf16[448,4096]{1,0:T(8,128)(2,1)} reshape(bf16[7,64,64,64]{3,2,1,0:T(8,128)(2,1)} %copy.12) | data formatting | bytes 7340032 | tf_op jit(solution)/shard_map/reshape | solution.py:62
  73.9 10.6 %reshape.51 = bf16[448,4096]{1,0:T(8,128)(2,1)} reshape(bf16[7,64,64,64]{3,2,1,0:T(8,128)(2,1)} %convert_bitcast_fusion.4) | data formatting | bytes 7340032 | tf_op jit(solution)/shard_map/reshape | solution.py:62
  88.1 5.6 %convert_bitcast_fusion.3 = bf16[7,64,64,64]{1,2,3,0:T(8,128)(2,1)} fusion(bf16[7,20,64,64]{3,2,0,1:T(8,128)(2,1)S(1)} %reshape_squeeze.11, s32[7,20]{1,0:T(8,128)S(1)} %bitcast.248), kind=kOutput, calls=%fused_computation.3 | convolution fusion | flops 75244288 | bytes 4817456 | tf_op jit(solution)/shard_map/crq,crkj->cjqk/dot_general | solution.py:61
  93.7 13.1 %copy.19 = bf16[7,64,64,64]{3,2,1,0:T(8,128)(2,1)} copy(bf16[7,64,64,64]{1,2,3,0:T(8,128)(2,1)} %convert_bitcast_fusion.3) | data formatting | bytes 7340032 | tf_op jit(solution)/shard_map/convert_element_type | solution.py:62
  106.8 10.6 %reshape.52 = bf16[448,4096]{1,0:T(8,128)(2,1)} reshape(bf16[7,64,64,64]{3,2,1,0:T(8,128)(2,1)} %copy.19) | data formatting | bytes 7340032 | tf_op jit(solution)/shard_map/reshape | solution.py:62
  118.3 4.5 %collective-permute-start.8 = (bf16[7,20,4096]{2,0,1:T(8,128)(2,1)}, bf16[7,20,4096]{2,0,1:T(8,128)(2,1)}, u32[]{:S(2)}, u32[]{:S(2)}) collective-permute-start(bf16[7,20,4096]{2,0,1:T(8,128)(2,1)} %bitcast.35), channel_id=1, source_target_pairs={{0,16},{16,0},{32,48},{48,32},{64,80},{80,64},{96,112},{112,96},{1... | collective-permute-start | bytes 3440648 | tf_op jit(solution)/shard_map/ppermute | solution.py:91
  130.9 5.6 %convert_bitcast_fusion.2 = bf16[7,64,64,64]{1,2,3,0:T(8,128)(2,1)} fusion(bf16[7,20,64,64]{3,2,0,1:T(8,128)(2,1)S(1)} %reshape.53, s32[7,20]{1,0:T(8,128)S(1)} %collective-permute-done.4), kind=kOutput, calls=%fused_computation.2 | convolution fusion | flops 75244288 | bytes 4817456 | tf_op jit(solution)/shard_map/crq,crkj->cjqk/dot_general | solution.py:61
  136.5 13.1 %copy.21 = bf16[7,64,64,64]{3,2,1,0:T(8,128)(2,1)} copy(bf16[7,64,64,64]{1,2,3,0:T(8,128)(2,1)} %convert_bitcast_fusion.2) | data formatting | bytes 7340032 | tf_op jit(solution)/shard_map/convert_element_type | solution.py:62
  149.7 10.6 %reshape.54 = bf16[448,4096]{1,0:T(8,128)(2,1)} reshape(bf16[7,64,64,64]{3,2,1,0:T(8,128)(2,1)} %copy.21) | data formatting | bytes 7340032 | tf_op jit(solution)/shard_map/reshape | solution.py:62
  163.8 5.5 %convert_bitcast_fusion.1 = bf16[7,64,64,64]{3,2,1,0:T(8,128)(2,1)} fusion(bf16[7,20,64,64]{3,2,0,1:T(8,128)(2,1)S(1)} %reshape.55, s32[7,20]{1,0:T(8,128)S(1)} %collective-permute-done.6), kind=kOutput, calls=%fused_computation.1 | convolution fusion | flops 75244288 | bytes 4817456 | tf_op jit(solution)/shard_map/crq,crjk->cjqk/dot_general | solution.py:61
  169.3 10.6 %reshape.56 = bf16[448,4096]{1,0:T(8,128)(2,1)} reshape(bf16[7,64,64,64]{3,2,1,0:T(8,128)(2,1)} %convert_bitcast_fusion.1) | data formatting | bytes 7340032 | tf_op jit(solution)/shard_map/reshape | solution.py:62
  183.5 5.6 %convert_bitcast_fusion = bf16[7,64,64,64]{1,2,3,0:T(8,128)(2,1)} fusion(bf16[7,20,64,64]{3,2,0,1:T(8,128)(2,1)S(1)} %reshape.57, s32[7,20]{1,0:T(8,128)S(1)} %collective-permute-done.4), kind=kOutput, calls=%fused_computation | convolution fusion | flops 75244288 | bytes 4817456 | tf_op jit(solution)/shard_map/crq,crkj->cjqk/dot_general | solution.py:61
  189.1 13.1 %copy.24 = bf16[7,64,64,64]{3,2,1,0:T(8,128)(2,1)} copy(bf16[7,64,64,64]{1,2,3,0:T(8,128)(2,1)} %convert_bitcast_fusion) | data formatting | bytes 7340032 | tf_op jit(solution)/shard_map/convert_element_type | solution.py:62
  202.2 10.7 %reshape.58 = bf16[448,4096]{1,0:T(8,128)(2,1)} reshape(bf16[7,64,64,64]{3,2,1,0:T(8,128)(2,1)} %copy.24) | data formatting | bytes 7340032 | tf_op jit(solution)/shard_map/reshape | solution.py:62
  219.7 8.8 %fusion.20 = f32[4096,128]{1,0:T(8,128)} fusion(bf16[448,4096]{1,0:T(8,128)(2,1)} %reshape.50, f32[448,128]{1,0:T(8,128)S(1)} %fusion.73, bf16[448,4096]{1,0:T(8,128)(2,1)} %reshape.52, bf16[4096,128]{1,0:T(8,128)(2,1)S(1)} %bitcast.232, f32[448,128]{1,0:T(8,128)S(1)} %fusion.74), kind=kOutput, calls=%fused_computation.35 | convolution fusion | flops 940097536 | bytes 10944512 | tf_op jit(solution)/shard_map/dot_general | solution.py:83
  236.6 8.9 %fusion.21 = f32[4096,128]{1,0:T(8,128)} fusion(bf16[448,4096]{1,0:T(8,128)(2,1)} %reshape.54, f32[448,128]{1,0:T(8,128)S(1)} %fusion.75, bf16[448,4096]{1,0:T(8,128)(2,1)} %reshape.58, bf16[4096,128]{1,0:T(8,128)(2,1)S(1)} %bitcast.234, f32[448,128]{1,0:T(8,128)} %fusion.76), kind=kOutput, calls=%fused_computation.36 | convolution fusion | flops 940097536 | bytes 10944512 | tf_op jit(solution)/shard_map/dot_general | solution.py:83
  259.3 5.4 %collective-permute-start.18 = (bf16[256,128]{1,0:T(8,128)(2,1)S(1)}, bf16[256,128]{1,0:T(8,128)(2,1)S(1)}, u32[]{:S(2)}, u32[]{:S(2)}) collective-permute-start(bf16[256,128]{1,0:T(8,128)(2,1)S(1)} %get-tuple-element.29), channel_id=1, source_target_pairs={{0,4},{1,5},{2,6},{3,7},{4,0},{5,1},{6,2},{7,3},{8,12},{9,13},{10,... | collective-permute-start | bytes 196616 | tf_op jit(solution)/shard_map/ppermute | solution.py:44
  277.5 6.0 %collective-permute-done.11 = f32[2,256,128]{2,1,0:T(8,128)S(1)} collective-permute-done((f32[2,256,128]{2,1,0:T(8,128)S(1)}, f32[2,256,128]{2,1,0:T(8,128)S(1)}, u32[]{:S(2)}, u32[]{:S(2)}) %collective-permute-start.11) | collective-permute-done | bytes 262176 | tf_op jit(solution)/shard_map/ppermute | solution.py:31
  283.5 5.4 %collective-permute-start.12 = (f32[256,128]{1,0:T(8,128)S(1)}, f32[256,128]{1,0:T(8,128)S(1)}, u32[]{:S(2)}, u32[]{:S(2)}) collective-permute-start(f32[256,128]{1,0:T(8,128)S(1)} %dynamic-slice_bitcast_fusion.7), channel_id=1, source_target_pairs={{0,4},{1,5},{2,6},{3,7},{4,0},{5,1},{6,2},{7,3},{8,12},{9,13},{10,... | collective-permute-start | bytes 393224 | tf_op jit(solution)/shard_map/ppermute | solution.py:31
  293.2 4.6 %collective-permute-done.20 = bf16[2,2,256,128]{3,2,1,0:T(8,128)(2,1)S(1)} collective-permute-done((bf16[2,2,256,128]{3,2,1,0:T(8,128)(2,1)S(1)}, bf16[2,2,256,128]{3,2,1,0:T(8,128)(2,1)S(1)}, u32[]{:S(2)}, u32[]{:S(2)}) %collective-permute-start.20) | collective-permute-done | bytes 262176 | tf_op jit(solution)/shard_map/ppermute | solution.py:44
  298.1 5.4 %collective-permute-start.14 = (bf16[256,128]{1,0:T(8,128)(2,1)S(1)}, bf16[256,128]{1,0:T(8,128)(2,1)S(1)}, u32[]{:S(2)}, u32[]{:S(2)}) collective-permute-start(bf16[256,128]{1,0:T(8,128)(2,1)S(1)} %bitcast_select_fusion), channel_id=1, source_target_pairs={{0,4},{1,5},{2,6},{3,7},{4,0},{5,1},{6,2},{7,3},{8,12},{9,13},{10,... | collective-permute-start | bytes 196616 | tf_op jit(solution)/shard_map/ppermute | solution.py:44
  316.2 6.8 %collective-permute-done.16 = bf16[2,2,256,128]{3,2,1,0:T(8,128)(2,1)S(1)} collective-permute-done((bf16[2,2,256,128]{3,2,1,0:T(8,128)(2,1)S(1)}, bf16[2,2,256,128]{3,2,1,0:T(8,128)(2,1)S(1)}, u32[]{:S(2)}, u32[]{:S(2)}) %collective-permute-start.16) | collective-permute-done | bytes 262176 | tf_op jit(solution)/shard_map/ppermute | solution.py:44
  332.3 8.8 %fusion.22 = f32[4096,128]{1,0:T(8,128)} fusion(bf16[448,4096]{1,0:T(8,128)(2,1)} %reshape.50, f32[448,128]{1,0:T(8,128)S(1)} %fusion.77, bf16[448,4096]{1,0:T(8,128)(2,1)} %reshape.52, bf16[4096,128]{1,0:T(8,128)(2,1)S(1)} %bitcast.229, f32[448,128]{1,0:T(8,128)S(1)} %fusion.78), kind=kOutput, calls=%fused_computation.37 | convolution fusion | flops 940097536 | bytes 10944512 | tf_op jit(solution)/shard_map/dot_general | solution.py:83
  345.3 8.7 %fusion.23 = f32[4096,128]{1,0:T(8,128)} fusion(bf16[448,4096]{1,0:T(8,128)(2,1)} %reshape.54, f32[448,128]{1,0:T(8,128)} %fusion.79, bf16[448,4096]{1,0:T(8,128)(2,1)} %reshape.58, bf16[4096,128]{1,0:T(8,128)(2,1)S(1)} %bitcast.230, f32[448,128]{1,0:T(8,128)S(1)} %fusion.80), kind=kOutput, calls=%fused_computation.38 | convolution fusion | flops 940097536 | bytes 10944512 | tf_op jit(solution)/shard_map/dot_general | solution.py:83
  365.4 13.9 %collective-permute-done.23 = f32[2,2,256,128]{3,2,1,0:T(8,128)S(1)} collective-permute-done((f32[2,2,256,128]{3,2,1,0:T(8,128)S(1)}, f32[2,2,256,128]{3,2,1,0:T(8,128)S(1)}, u32[]{:S(2)}, u32[]{:S(2)}) %collective-permute-start.23) | collective-permute-done | bytes 524320 | tf_op jit(solution)/shard_map/ppermute | solution.py:31
  381.7 7.3 %collective-permute-done.24 = f32[2,256,128]{2,1,0:T(8,128)S(1)} collective-permute-done((f32[2,256,128]{2,1,0:T(8,128)S(1)}, f32[2,256,128]{2,1,0:T(8,128)S(1)}, u32[]{:S(2)}, u32[]{:S(2)}) %collective-permute-start.24) | collective-permute-done | bytes 262176 | tf_op jit(solution)/shard_map/ppermute | solution.py:31
  392.5 4.9 %collective-permute-done.25 = f32[256,128]{1,0:T(8,128)S(1)} collective-permute-done((f32[256,128]{1,0:T(8,128)S(1)}, f32[256,128]{1,0:T(8,128)S(1)}, u32[]{:S(2)}, u32[]{:S(2)}) %collective-permute-start.25) | collective-permute-done | bytes 131104 | tf_op jit(solution)/shard_map/ppermute | solution.py:31
  (150 shorter events, 137.1 us)
Async XLA Ops:
  1.8 29.3 %collective-permute-start = (bf16[2,256,128]{2,1,0:T(8,128)(2,1)S(1)}, bf16[2,256,128]{2,1,0:T(8,128)(2,1)S(1)}, u32[]{:S(2)}, u32[]{:S(2)}) collective-permute-start(bf16[2,256,128]{2,1,0:T(8,128)(2,1)S(1)} %pad_maximum_fusion.7), channel_id=1, source_target_pairs={{0,4},{1,5},{2,6},{3,7},{4,0},{5,1},{6,2},{7,3},{8,12},{9,13},{10,... | collective-permute-start | bytes 393224 | tf_op jit(solution)/shard_map/ppermute | solution.py:44
  6.9 118.2 %collective-permute-start.5 = (bf16[7,20,4096]{2,0,1:T(8,128)(2,1)}, bf16[7,20,4096]{2,0,1:T(8,128)(2,1)}, u32[]{:S(2)}, u32[]{:S(2)}) collective-permute-start(bf16[7,20,4096]{2,0,1:T(8,128)(2,1)} %bitcast.243), channel_id=1, source_target_pairs={{0,16},{16,0},{32,48},{48,32},{64,80},{80,64},{96,112},{112,96},{1... | collective-permute-start | bytes 3440648 | tf_op jit(solution)/shard_map/ppermute | solution.py:91
  10.9 120.1 %collective-permute-start.4 = (s32[7,20]{1,0:T(8,128)S(1)}, s32[7,20]{1,0:T(8,128)S(1)}, u32[]{:S(2)}, u32[]{:S(2)}) collective-permute-start(s32[7,20]{1,0:T(8,128)S(1)} %bitcast.246), channel_id=1, source_target_pairs={{0,16},{16,0},{32,48},{48,32},{64,80},{80,64},{96,112},{112,96},{1... | collective-permute-start | bytes 1688 | tf_op jit(solution)/shard_map/ppermute | solution.py:91
  14.9 145.3 %collective-permute-start.7 = (bf16[7,20,4096]{2,0,1:T(8,128)(2,1)}, bf16[7,20,4096]{2,0,1:T(8,128)(2,1)}, u32[]{:S(2)}, u32[]{:S(2)}) collective-permute-start(bf16[7,20,4096]{2,0,1:T(8,128)(2,1)} %bitcast.244), channel_id=1, source_target_pairs={{0,16},{16,0},{32,48},{48,32},{64,80},{80,64},{96,112},{112,96},{1... | collective-permute-start | bytes 3440648 | tf_op jit(solution)/shard_map/ppermute | solution.py:91
  18.9 144.9 %collective-permute-start.6 = (s32[7,20]{1,0:T(8,128)S(1)}, s32[7,20]{1,0:T(8,128)S(1)}, u32[]{:S(2)}, u32[]{:S(2)}) collective-permute-start(s32[7,20]{1,0:T(8,128)S(1)} %bitcast.249), channel_id=1, source_target_pairs={{0,16},{16,0},{32,48},{48,32},{64,80},{80,64},{96,112},{112,96},{1... | collective-permute-start | bytes 1688 | tf_op jit(solution)/shard_map/ppermute | solution.py:91
  31.2 9.7 %collective-permute-start.1 = (bf16[2,2,256,128]{3,2,1,0:T(8,128)(2,1)S(1)}, bf16[2,2,256,128]{3,2,1,0:T(8,128)(2,1)S(1)}, u32[]{:S(2)}, u32[]{:S(2)}) collective-permute-start(bf16[2,2,256,128]{3,2,1,0:T(8,128)(2,1)S(1)} %pad_maximum_fusion.4), channel_id=1, source_target_pairs={{0,2},{1,3},{2,0},{3,1},{4,6},{5,7},{6,4},{7,5},{8,10},{9,11},{10,... | collective-permute-start | bytes 786440 | tf_op jit(solution)/shard_map/ppermute | solution.py:44
  41.7 75.7 %collective-permute-start.2 = (bf16[2,2,2,256,128]{4,3,1,2,0:T(8,128)(2,1)S(1)}, bf16[2,2,2,256,128]{4,3,1,2,0:T(8,128)(2,1)S(1)}, u32[]{:S(2)}, u32[]{:S(2)}) collective-permute-start(bf16[2,2,2,256,128]{4,3,1,2,0:T(8,128)(2,1)S(1)} %pad_maximum_fusion.1), channel_id=1, source_target_pairs={{0,8},{1,9},{2,10},{3,11},{4,12},{5,13},{6,14},{7,15},{8,0},{9,1},... | collective-permute-start | bytes 1572872 | tf_op jit(solution)/shard_map/ppermute | solution.py:44
  106.8 16.0 %copy-start.12 = (bf16[2,1,2,256,128]{4,3,1,2,0:T(8,128)(2,1)S(1)}, bf16[2,1,2,256,128]{4,3,1,2,0:T(8,128)(2,1)}, u32[]{:S(2)}) copy-start(bf16[2,1,2,256,128]{4,3,1,2,0:T(8,128)(2,1)} %copy-done.11) | copy-start | bytes 786436
  106.8 16.0 %copy-start.14 = (bf16[2,1,2,256,128]{4,3,1,2,0:T(8,128)(2,1)S(1)}, bf16[2,1,2,256,128]{4,3,1,2,0:T(8,128)(2,1)}, u32[]{:S(2)}) copy-start(bf16[2,1,2,256,128]{4,3,1,2,0:T(8,128)(2,1)} %copy-done.13) | copy-start | bytes 786436
  118.3 61.7 %collective-permute-start.8 = (bf16[7,20,4096]{2,0,1:T(8,128)(2,1)}, bf16[7,20,4096]{2,0,1:T(8,128)(2,1)}, u32[]{:S(2)}, u32[]{:S(2)}) collective-permute-start(bf16[7,20,4096]{2,0,1:T(8,128)(2,1)} %bitcast.35), channel_id=1, source_target_pairs={{0,16},{16,0},{32,48},{48,32},{64,80},{80,64},{96,112},{112,96},{1... | collective-permute-start | bytes 3440648 | tf_op jit(solution)/shard_map/ppermute | solution.py:91
  125.0 87.9 %collective-permute-start.3 = (bf16[2,2,2,2,256,128]{5,4,2,3,1,0:T(8,128)(2,1)}, bf16[2,2,2,2,256,128]{5,4,2,3,1,0:T(8,128)(2,1)}, u32[]{:S(2)}, u32[]{:S(2)}) collective-permute-start(bf16[2,2,2,2,256,128]{5,4,2,3,1,0:T(8,128)(2,1)} %pad_maximum_fusion), channel_id=1, source_target_pairs={{0,1},{1,0},{2,3},{3,2},{4,5},{5,4},{6,7},{7,6},{8,9},{9,8},{10,11... | collective-permute-start | bytes 3145736 | tf_op jit(solution)/shard_map/ppermute | solution.py:44
  249.8 17.6 %copy-start.20 = (bf16[1,2,256,128]{3,2,1,0:T(8,128)(2,1)S(1)}, bf16[1,2,256,128]{3,2,1,0:T(8,128)(2,1)}, u32[]{:S(2)}) copy-start(bf16[1,2,256,128]{3,2,1,0:T(8,128)(2,1)} %param.7) | copy-start | bytes 393220
  251.3 4.7 %collective-permute-start.9 = (f32[2,2,2,256,128]{4,3,2,1,0:T(8,128)S(1)}, f32[2,2,2,256,128]{4,3,2,1,0:T(8,128)S(1)}, u32[]{:S(2)}, u32[]{:S(2)}) collective-permute-start(f32[2,2,2,256,128]{4,3,2,1,0:T(8,128)S(1)} %dynamic-slice_bitcast_fusion.1), channel_id=1, source_target_pairs={{0,1},{1,0},{2,3},{3,2},{4,5},{5,4},{6,7},{7,6},{8,9},{9,8},{10,11... | collective-permute-start | bytes 3145736 | tf_op jit(solution)/shard_map/ppermute | solution.py:31
  257.3 34.6 %copy-start.19 = (bf16[1,2,256,128]{3,2,1,0:T(8,128)(2,1)S(1)}, bf16[1,2,256,128]{3,2,1,0:T(8,128)(2,1)}, u32[]{:S(2)}) copy-start(bf16[1,2,256,128]{3,2,1,0:T(8,128)(2,1)} %param.8) | copy-start | bytes 393220
  257.3 16.1 %collective-permute-start.10 = (f32[2,2,256,128]{3,2,1,0:T(8,128)S(1)}, f32[2,2,256,128]{3,2,1,0:T(8,128)S(1)}, u32[]{:S(2)}, u32[]{:S(2)}) collective-permute-start(f32[2,2,256,128]{3,2,1,0:T(8,128)S(1)} %dynamic-slice_bitcast_fusion.3), channel_id=1, source_target_pairs={{0,8},{1,9},{2,10},{3,11},{4,12},{5,13},{6,14},{7,15},{8,0},{9,1},... | collective-permute-start | bytes 1572872 | tf_op jit(solution)/shard_map/ppermute | solution.py:31
  259.3 8.0 %collective-permute-start.18 = (bf16[256,128]{1,0:T(8,128)(2,1)S(1)}, bf16[256,128]{1,0:T(8,128)(2,1)S(1)}, u32[]{:S(2)}, u32[]{:S(2)}) collective-permute-start(bf16[256,128]{1,0:T(8,128)(2,1)S(1)} %get-tuple-element.29), channel_id=1, source_target_pairs={{0,4},{1,5},{2,6},{3,7},{4,0},{5,1},{6,2},{7,3},{8,12},{9,13},{10,... | collective-permute-start | bytes 196616 | tf_op jit(solution)/shard_map/ppermute | solution.py:44
  267.4 10.1 %collective-permute-start.19 = (bf16[2,256,128]{2,1,0:T(8,128)(2,1)S(1)}, bf16[2,256,128]{2,1,0:T(8,128)(2,1)S(1)}, u32[]{:S(2)}, u32[]{:S(2)}) collective-permute-start(bf16[2,256,128]{2,1,0:T(8,128)(2,1)S(1)} %pad_maximum_fusion.9), channel_id=1, source_target_pairs={{0,2},{1,3},{2,0},{3,1},{4,6},{5,7},{6,4},{7,5},{8,10},{9,11},{10,... | collective-permute-start | bytes 393224 | tf_op jit(solution)/shard_map/ppermute | solution.py:44
  273.5 9.9 %collective-permute-start.11 = (f32[2,256,128]{2,1,0:T(8,128)S(1)}, f32[2,256,128]{2,1,0:T(8,128)S(1)}, u32[]{:S(2)}, u32[]{:S(2)}) collective-permute-start(f32[2,256,128]{2,1,0:T(8,128)S(1)} %dynamic-slice_bitcast_fusion.5), channel_id=1, source_target_pairs={{0,2},{1,3},{2,0},{3,1},{4,6},{5,7},{6,4},{7,5},{8,10},{9,11},{10,... | collective-permute-start | bytes 786440 | tf_op jit(solution)/shard_map/ppermute | solution.py:31
  283.5 8.4 %collective-permute-start.12 = (f32[256,128]{1,0:T(8,128)S(1)}, f32[256,128]{1,0:T(8,128)S(1)}, u32[]{:S(2)}, u32[]{:S(2)}) collective-permute-start(f32[256,128]{1,0:T(8,128)S(1)} %dynamic-slice_bitcast_fusion.7), channel_id=1, source_target_pairs={{0,4},{1,5},{2,6},{3,7},{4,0},{5,1},{6,2},{7,3},{8,12},{9,13},{10,... | collective-permute-start | bytes 393224 | tf_op jit(solution)/shard_map/ppermute | solution.py:31
  289.0 8.8 %collective-permute-start.20 = (bf16[2,2,256,128]{3,2,1,0:T(8,128)(2,1)S(1)}, bf16[2,2,256,128]{3,2,1,0:T(8,128)(2,1)S(1)}, u32[]{:S(2)}, u32[]{:S(2)}) collective-permute-start(bf16[2,2,256,128]{3,2,1,0:T(8,128)(2,1)S(1)} %pad_maximum_fusion.6), channel_id=1, source_target_pairs={{0,8},{1,9},{2,10},{3,11},{4,12},{5,13},{6,14},{7,15},{8,0},{9,1},... | collective-permute-start | bytes 786440 | tf_op jit(solution)/shard_map/ppermute | solution.py:44
  291.9 6.2 %collective-permute-start.13 = (bf16[256,128]{1,0:T(8,128)(2,1)S(1)}, bf16[256,128]{1,0:T(8,128)(2,1)S(1)}, u32[]{:S(2)}, u32[]{:S(2)}) collective-permute-start(bf16[256,128]{1,0:T(8,128)(2,1)S(1)} %fusion.36), channel_id=1, source_target_pairs={{32,0},{48,16},{64,32},{80,48},{96,64},{112,80},{128,96},{144,112}... | collective-permute-start | bytes 196616 | tf_op jit(solution)/shard_map/ppermute | solution.py:17
  298.1 7.7 %collective-permute-start.14 = (bf16[256,128]{1,0:T(8,128)(2,1)S(1)}, bf16[256,128]{1,0:T(8,128)(2,1)S(1)}, u32[]{:S(2)}, u32[]{:S(2)}) collective-permute-start(bf16[256,128]{1,0:T(8,128)(2,1)S(1)} %bitcast_select_fusion), channel_id=1, source_target_pairs={{0,4},{1,5},{2,6},{3,7},{4,0},{5,1},{6,2},{7,3},{8,12},{9,13},{10,... | collective-permute-start | bytes 196616 | tf_op jit(solution)/shard_map/ppermute | solution.py:44
  303.6 12.3 %collective-permute-start.21 = (bf16[2,2,2,256,128]{4,3,2,1,0:T(8,128)(2,1)S(1)}, bf16[2,2,2,256,128]{4,3,2,1,0:T(8,128)(2,1)S(1)}, u32[]{:S(2)}, u32[]{:S(2)}) collective-permute-start(bf16[2,2,2,256,128]{4,3,2,1,0:T(8,128)(2,1)S(1)} %pad_maximum_fusion.3), channel_id=1, source_target_pairs={{0,1},{1,0},{2,3},{3,2},{4,5},{5,4},{6,7},{7,6},{8,9},{9,8},{10,11... | collective-permute-start | bytes 1572872 | tf_op jit(solution)/shard_map/ppermute | solution.py:44
  305.8 7.6 %collective-permute-start.15 = (bf16[2,256,128]{2,1,0:T(8,128)(2,1)S(1)}, bf16[2,256,128]{2,1,0:T(8,128)(2,1)S(1)}, u32[]{:S(2)}, u32[]{:S(2)}) collective-permute-start(bf16[2,256,128]{2,1,0:T(8,128)(2,1)S(1)} %pad_maximum_fusion.8), channel_id=1, source_target_pairs={{0,2},{1,3},{2,0},{3,1},{4,6},{5,7},{6,4},{7,5},{8,10},{9,11},{10,... | collective-permute-start | bytes 393224 | tf_op jit(solution)/shard_map/ppermute | solution.py:44
  313.4 9.6 %collective-permute-start.16 = (bf16[2,2,256,128]{3,2,1,0:T(8,128)(2,1)S(1)}, bf16[2,2,256,128]{3,2,1,0:T(8,128)(2,1)S(1)}, u32[]{:S(2)}, u32[]{:S(2)}) collective-permute-start(bf16[2,2,256,128]{3,2,1,0:T(8,128)(2,1)S(1)} %pad_maximum_fusion.5), channel_id=1, source_target_pairs={{0,8},{1,9},{2,10},{3,11},{4,12},{5,13},{6,14},{7,15},{8,0},{9,1},... | collective-permute-start | bytes 786440 | tf_op jit(solution)/shard_map/ppermute | solution.py:44
  316.0 9.1 %copy-start.1 = (bf16[448,4096]{1,0:T(8,128)(2,1)S(1)}, bf16[448,4096]{1,0:T(8,128)(2,1)}, u32[]{:S(2)}) copy-start(bf16[448,4096]{1,0:T(8,128)(2,1)} %reshape.50) | copy-start | bytes 11010052
  316.2 10.0 %copy-start.3 = (bf16[448,4096]{1,0:T(8,128)(2,1)S(1)}, bf16[448,4096]{1,0:T(8,128)(2,1)}, u32[]{:S(2)}) copy-start(bf16[448,4096]{1,0:T(8,128)(2,1)} %reshape.54) | copy-start | bytes 11010052
  323.1 4.2 %collective-permute-start.17 = (bf16[2,2,2,256,128]{4,3,2,1,0:T(8,128)(2,1)S(1)}, bf16[2,2,2,256,128]{4,3,2,1,0:T(8,128)(2,1)S(1)}, u32[]{:S(2)}, u32[]{:S(2)}) collective-permute-start(bf16[2,2,2,256,128]{4,3,2,1,0:T(8,128)(2,1)S(1)} %pad_maximum_fusion.2), channel_id=1, source_target_pairs={{0,1},{1,0},{2,3},{3,2},{4,5},{5,4},{6,7},{7,6},{8,9},{9,8},{10,11... | collective-permute-start | bytes 1572872 | tf_op jit(solution)/shard_map/ppermute | solution.py:44
  358.3 4.7 %collective-permute-start.22 = (f32[2,2,2,256,128]{4,3,2,1,0:T(8,128)S(1)}, f32[2,2,2,256,128]{4,3,2,1,0:T(8,128)S(1)}, u32[]{:S(2)}, u32[]{:S(2)}) collective-permute-start(f32[2,2,2,256,128]{4,3,2,1,0:T(8,128)S(1)} %dynamic-slice_bitcast_fusion), channel_id=1, source_target_pairs={{0,1},{1,0},{2,3},{3,2},{4,5},{5,4},{6,7},{7,6},{8,9},{9,8},{10,11... | collective-permute-start | bytes 3145736 | tf_op jit(solution)/shard_map/ppermute | solution.py:31
  363.2 16.1 %collective-permute-start.23 = (f32[2,2,256,128]{3,2,1,0:T(8,128)S(1)}, f32[2,2,256,128]{3,2,1,0:T(8,128)S(1)}, u32[]{:S(2)}, u32[]{:S(2)}) collective-permute-start(f32[2,2,256,128]{3,2,1,0:T(8,128)S(1)} %dynamic-slice_bitcast_fusion.2), channel_id=1, source_target_pairs={{0,8},{1,9},{2,10},{3,11},{4,12},{5,13},{6,14},{7,15},{8,0},{9,1},... | collective-permute-start | bytes 1572872 | tf_op jit(solution)/shard_map/ppermute | solution.py:31
  379.4 9.7 %collective-permute-start.24 = (f32[2,256,128]{2,1,0:T(8,128)S(1)}, f32[2,256,128]{2,1,0:T(8,128)S(1)}, u32[]{:S(2)}, u32[]{:S(2)}) collective-permute-start(f32[2,256,128]{2,1,0:T(8,128)S(1)} %dynamic-slice_bitcast_fusion.4), channel_id=1, source_target_pairs={{0,2},{1,3},{2,0},{3,1},{4,6},{5,7},{6,4},{7,5},{8,10},{9,11},{10,... | collective-permute-start | bytes 786440 | tf_op jit(solution)/shard_map/ppermute | solution.py:31
  389.1 8.4 %collective-permute-start.25 = (f32[256,128]{1,0:T(8,128)S(1)}, f32[256,128]{1,0:T(8,128)S(1)}, u32[]{:S(2)}, u32[]{:S(2)}) collective-permute-start(f32[256,128]{1,0:T(8,128)S(1)} %dynamic-slice_bitcast_fusion.6), channel_id=1, source_target_pairs={{0,4},{1,5},{2,6},{3,7},{4,0},{5,1},{6,2},{7,3},{8,12},{9,13},{10,... | collective-permute-start | bytes 393224 | tf_op jit(solution)/shard_map/ppermute | solution.py:31
  (15 other events, 36.8 us)
